TPU v7x, 32 devices: a whole 2x2x4 slice. The times are simulated.
32 devices in a mesh: dp: 8 (over z, x), mp: 4 (over y, core).
Axes of the slice: x: 2, y: 2, z: 4, core: 2. Of those that a mesh axis runs over, the one named last changes fastest.
Arguments:
- queries: bfloat16 [1024, 4, 8192], P('dp', None, 'mp'), may hold values from -6 to 6
- fresh_key_value: bfloat16 [1024, 4, 2, 8, 128], P('dp', None, None, 'mp'), may hold values from -6 to 6
- key_value_pool: bfloat16 [4096, 2, 8, 16, 128], P('dp', None, 'mp'), may hold values from -6 to 6
- block_position_map: int32 [4096], replicated, may hold values from 0 to 4095
- request_blocks: int32 [1024, 4], P('dp'), may hold values from 0 to 4095, as said below
- live_prefix_length: int32 [1024], P('dp'), may hold values from 1 to 64, as said below
- request_adapter: int32 [1024, 1], P('dp'), may hold values from 0 to 15; in each aligned block of 128 rows (0 to 127, 128 to 255, ...) at most 8 rows name the same one
- output_weight: bfloat16 [8192, 8192], P('mp'), may hold values from -0.0625 to 0.0625
- adapter_down_panels: bfloat16 [16, 64, 8192], P('dp', None, 'mp'), may hold values from -0.0625 to 0.0625
- adapter_up_panels: bfloat16 [16, 64, 8192], P('dp', None, 'mp'), may hold values from -0.75 to 0.75
Outputs:
- layer_out: bfloat16 [1024, 4, 8192], P('dp', None, 'mp')
Inputs may be any that keep to these rules, and one draw needn't show every extreme that they name: `request_blocks`: every logical block is given a distinct pool position. The 512 entries of one index of dp name 256 distinct blocks, each exactly twice. Through the owner map at most 64 distinct blocks of one index of dp, and so at most 128 of its entries, lie on one pool owner (pool positions owner * 512 to owner * 512 + 511); one pool owner holds exactly 64 distinct blocks of every index of dp. `live_prefix_length`: all requests of some index of dp have the full 4 * 16 prefix tokens. `request_adapter`: among the 128 requests of one index of dp no adapter appears more than 8 times, and that many is reached.
All inputs are finite; a program needn't handle non-finite values.
Results may differ from a plain program's by a relative error of at most 0.008.
Values may be sent and summed in bfloat16 or wider, within the bound.
No kernel may reach another device: no remote copies, remote signals or barrier semaphores. Data moves between devices by JAX's collectives and lax.ppermute only.
A program may use at most 192 MiB of HBM per device.

v0:
```python
import jax
import jax.numpy as jnp
from jax import lax
from jax.sharding import PartitionSpec as P

ADAPTER_SCALE = 2.0


def shards(
    queries,
    fresh_key_value,
    key_value_pool,
    block_position_map,
    request_blocks,
    live_prefix_length,
    request_adapter,
    output_weight,
    adapter_down_panels,
    adapter_up_panels,
):
    owners = lax.axis_size("dp")
    req_dev, step_count, query_width = queries.shape
    kv_heads = fresh_key_value.shape[3]
    head_dim = fresh_key_value.shape[4]
    pool_dev = key_value_pool.shape[0]
    block_len = key_value_pool.shape[3]
    blocks_per = request_blocks.shape[1]
    entries = req_dev * blocks_per
    out_width = output_weight.shape[1]
    owner_range = jnp.arange(owners)
    positions = jnp.take(block_position_map, request_blocks.reshape(entries))
    target = positions // pool_dev
    local_slot = positions % pool_dev
    capacity = entries // owners
    entry_ids = jnp.arange(entries)
    same_block = positions[:, None] == positions[None, :]
    earlier = entry_ids[None, :] < entry_ids[:, None]
    first = jnp.logical_not(jnp.any(same_block & earlier, axis=1))
    same_owner = target[:, None] == target[None, :]
    rank = jnp.sum((same_owner & earlier & first[None, :]).astype(jnp.int32), axis=1)
    first_of = same_block & first[None, :]
    slot_index = jnp.sum(jnp.where(first_of, rank[None, :], 0), axis=1)
    key = jnp.where(first, target * capacity + rank, -1)
    table_ids = jnp.arange(owners * capacity)
    wish_table = jnp.sum(
        jnp.where(key[:, None] == table_ids[None, :], local_slot[:, None], 0), axis=0
    ).reshape(owners, capacity)
    wanted = lax.all_to_all(wish_table, "dp", split_axis=0, concat_axis=0, tiled=True)
    served = jnp.take(key_value_pool, wanted.reshape(-1), axis=0).reshape(
        (owners, capacity) + key_value_pool.shape[1:]
    )
    fetched = lax.all_to_all(served, "dp", split_axis=0, concat_axis=0, tiled=True)
    flat_rows = fetched.reshape((owners * capacity,) + key_value_pool.shape[1:])
    own_blocks = jnp.take(flat_rows, target * capacity + slot_index, axis=0)
    own_blocks = own_blocks.reshape((req_dev, blocks_per) + key_value_pool.shape[1:])
    group_size = query_width // (kv_heads * head_dim)
    query = queries.reshape(req_dev, step_count, kv_heads, group_size, head_dim)
    score_scale = head_dim ** (-0.5)
    prefix_scores = (
        jnp.einsum(
            "qsghd,qbgtd->qsghbt", query, own_blocks[:, :, 0], preferred_element_type=jnp.float32
        )
        * score_scale
    )
    token_index = jnp.arange(blocks_per)[:, None] * block_len + jnp.arange(block_len)[None, :]
    live_mask = token_index[None] < live_prefix_length[:, None, None]
    prefix_scores = jnp.where(live_mask[:, None, None, None], prefix_scores, -jnp.inf)
    fresh_scores = (
        jnp.einsum(
            "qsghd,qjgd->qsghj", query, fresh_key_value[:, :, 0], preferred_element_type=jnp.float32
        )
        * score_scale
    )
    causal = jnp.arange(step_count)[None, :] <= jnp.arange(step_count)[:, None]
    fresh_scores = jnp.where(causal[None, :, None, None, :], fresh_scores, -jnp.inf)
    row_top = jnp.maximum(jnp.max(prefix_scores, axis=(4, 5)), jnp.max(fresh_scores, axis=4))
    prefix_w = jnp.exp(prefix_scores - row_top[..., None, None])
    fresh_w = jnp.exp(fresh_scores - row_top[..., None])
    row_total = jnp.sum(prefix_w, axis=(4, 5)) + jnp.sum(fresh_w, axis=4)
    prefix_p = (prefix_w / row_total[..., None, None]).astype(jnp.bfloat16)
    fresh_p = (fresh_w / row_total[..., None]).astype(jnp.bfloat16)
    attended = jnp.einsum(
        "qsghbt,qbgtd->qsghd", prefix_p, own_blocks[:, :, 1], preferred_element_type=jnp.float32
    )
    attended = attended + jnp.einsum(
        "qsghj,qjgd->qsghd", fresh_p, fresh_key_value[:, :, 1], preferred_element_type=jnp.float32
    )
    attended = attended.astype(jnp.bfloat16).reshape(req_dev, step_count, query_width)
    base_product = jnp.dot(
        attended.reshape(req_dev * step_count, query_width),
        output_weight,
        preferred_element_type=jnp.float32,
    )
    base_product = base_product.reshape(req_dev, step_count, out_width)
    adapter = request_adapter[:, 0]
    single_panel = lax.all_gather(adapter_down_panels, "dp", axis=0, tiled=True)
    panel_count = single_panel.shape[0]
    hit_mask = (adapter[:, None] == jnp.arange(panel_count)[None, :]).astype(jnp.float32)
    every_rank = jnp.einsum(
        "qsf,nrf->qsnr", attended, single_panel, preferred_element_type=jnp.float32
    )
    rank_part = jnp.einsum("qsnr,qn->qsr", every_rank, hit_mask)
    rank_sum = lax.psum(rank_part, "mp").astype(jnp.bfloat16)
    single_panel = lax.all_gather(adapter_up_panels, "dp", axis=0, tiled=True)
    panel_count = single_panel.shape[0]
    hit_mask = (adapter[:, None] == jnp.arange(panel_count)[None, :]).astype(jnp.bfloat16)
    selected_panel = rank_sum[:, :, None, :] * hit_mask[:, None, :, None]
    adapter_sum = jnp.einsum(
        "utja,jam->utm", selected_panel, single_panel, preferred_element_type=jnp.float32
    )
    adapter_output = (adapter_sum * ADAPTER_SCALE).astype(jnp.bfloat16)
    summed_output = lax.psum_scatter(base_product, "mp", scatter_dimension=2, tiled=True)
    return (summed_output + adapter_output.astype(jnp.float32)).astype(jnp.bfloat16)


def solution(mesh):
    in_specs = (
        P("dp", None, "mp"),
        P("dp", None, None, "mp", None),
        P("dp", None, "mp", None, None),
        P(),
        P("dp", None),
        P("dp"),
        P("dp", None),
        P("mp", None),
        P("dp", None, "mp"),
        P("dp", None, "mp"),
    )
    out_specs = P("dp", None, "mp")
    return jax.shard_map(shards, mesh=mesh, in_specs=in_specs, out_specs=out_specs, check_vma=False)
```

profile of v0, /device:TPU:0, one launch (start us, length us, event | category | flops | bytes accessed | tf_op | source)
XLA Modules:
  0.0 584.8 jit_solution(10500240088412221773)
XLA Ops:
  7.4 0.8 copy.87
  8.4 3.1 gather_fusion
  12.4 13.5 %all_to_all.14 = s32[8,1,64]{2,1,0:T(1,128)S(1)} all-to-all(s32[8,1,64]{2,1,0:T(1,128)S(1)} %all_to_all.9), channel_id=1, replica_groups=mesh['dp'=8,'mp'=4] {'dp'}, dimensions={0} | all-to-all | bytes 4096 | tf_op jit(solution)/shard_map/all_to_all | solution.py:48
  26.5 0.7 reduce.5
  27.2 22.9 %gather_fusion.1 = bf16[512,2,2,16,128]{4,3,2,1,0:T(8,128)(2,1)} fusion(bf16[512,2,2,16,128]{4,3,2,1,0:T(8,128)(2,1)} %param.14, s32[1024]{0:T(1024)S(1)} %pad_clamp_fusion.1), kind=kCustom, calls=%fused_computation.clone | custom fusion | bytes 16779264 | tf_op jit(solution)/shard_map/jit(_take)/gather | solution.py:49
  50.1 7.6 %broadcast_select_fusion.1 = bf16[512,2,2,16,128]{4,3,2,1,0:T(8,128)(2,1)} fusion(bf16[512,2,2,16,128]{4,3,2,1,0:T(8,128)(2,1)} %gather_fusion.1, pred[512]{0:T(512)(128)(4,1)S(1)} %compare_and_fusion.3), kind=kLoop, calls=%fused_computation.6 | loop fusion | flops 4194304 | bytes 16777728 | tf_op jit(solution)/shard_map/jit(_take)/select_n | solution.py:49
  57.7 5.0 all-to-all-start.1
  62.7 0.7 all-gather.3.cloned.1.call-update
  63.5 0.7 all-gather.5.cloned.1.call-update
  64.4 3.2 reshape.275
  68.0 10.8 %fusion.37 = (f32[128,4,2,8]{3,1,2,0:T(4,128)S(1)}, f32[128,4,2,8,4]{3,4,1,2,0:T(4,128)}) fusion(bf16[128,4,2,8,128]{4,3,2,1,0:T(8,128)(2,1)S(1)} %reshape.275, bf16[128,4,1,2,128]{4,3,2,1,0:T(2,128)(2,1)S(1)} %get-tuple-element.13, pred[4,4]{1,0:T(4,128)(4,1)S(1)} %iota_compare_fusion.3), kind=kOutput, calls=%fused_computation.79 | convolution fusion | flops 8478720 | bytes 2523152 | tf_op jit(solution)/shard_map/qsghd,qjgd->qsghj/dot_general | solution.py:69
  79.5 232.6 %all-to-all-done.1 = bf16[8,64,2,2,16,128]{5,4,3,2,1,0:T(8,128)(2,1)} async-done(((bf16[8,64,2,2,16,128]{5,4,3,2,1,0:T(8,128)(2,1)}), bf16[8,64,2,2,16,128]{5,4,3,2,1,0:T(8,128)(2,1)}, u32[]{:S(2)}, u32[]{:S(2)}) %all-to-all-start.1) | async-done | bytes 8388640 | tf_op jit(solution)/shard_map/all_to_all | solution.py:52
  312.1 23.6 %gather_fusion.2 = bf16[512,2,2,16,128]{4,3,2,1,0:T(8,128)(2,1)} fusion(bf16[512,2,2,16,128]{4,3,2,1,0:T(8,128)(2,1)} %bitcast.3, s32[1024]{0:T(1024)S(1)} %pad_clamp_fusion), kind=kCustom, calls=%fused_computation.1.clone | custom fusion | bytes 16779264 | tf_op jit(solution)/shard_map/jit(_take)/gather | solution.py:54
  335.7 4.9 broadcast_select_fusion
  340.6 3.7 fusion.35
  344.3 17.3 %fusion.2 = f32[128,2,4,16,4,8]{3,5,4,2,1,0:T(8,128)} fusion(bf16[128,4,1,2,16,128]{5,4,3,2,1,0:T(8,128)(2,1)S(1)} %get-tuple-element.11, bf16[128,4,2,8,128]{4,3,2,1,0:T(8,128)(2,1)S(1)} %reshape.275), kind=kOutput, calls=%fused_computation.8 | convolution fusion | flops 134217728 | bytes 8388608 | tf_op jit(solution)/shard_map/qsghd,qbgtd->qsghbt/dot_general | solution.py:60
  361.6 12.2 %copy.92 = f32[128,2,4,16,4,8]{0,3,2,5,1,4:T(8,128)S(1)} copy(f32[128,2,4,16,4,8]{3,5,4,2,1,0:T(8,128)} %fusion.2) | data formatting | bytes 4194304 | tf_op jit(solution)/shard_map/qsghd,qbgtd->qsghbt/dot_general | solution.py:60
  374.5 3.6 fusion.22
  378.3 0.6 fusion.23
  378.9 1.1 copy.99
  380.0 0.6 divide_convert_fusion
  380.6 22.9 %copy.98 = bf16[128,4,2,8,4,16]{5,3,4,1,2,0:T(8,128)(2,1)} copy(bf16[128,4,2,8,4,16]{0,5,4,3,2,1:T(8,128)(2,1)S(1)} %divide_convert_fusion) | data formatting | bytes 2097152 | tf_op jit(solution)/shard_map/convert_element_type | solution.py:80
  403.5 7.0 %fusion.3 = f32[128,2,128,4,8,1]{2,4,5,3,1,0:T(8,128)S(1)} fusion(bf16[128,4,2,8,4,16]{5,3,4,1,2,0:T(8,128)(2,1)} %copy.98, bf16[128,4,1,2,16,128]{5,4,3,2,1,0:T(8,128)(2,1)} %get-tuple-element.10), kind=kOutput, calls=%fused_computation.10 | convolution fusion | flops 134217728 | bytes 9437184 | tf_op jit(solution)/shard_map/qsghbt,qbgtd->qsghd/dot_general | solution.py:82
  410.5 2.6 fusion.4
  413.1 3.4 copy.101
  416.6 27.0 %fusion = f32[128,4,8192]{2,0,1:T(8,128)} fusion(bf16[128,4,2048]{0,2,1:T(8,128)(2,1)S(1)} %bitcast.89, bf16[2048,8192]{1,0:T(8,128)(2,1)} %param.19), kind=kOutput, calls=%fused_computation.3 | convolution fusion | flops 17179869184 | bytes 52428800 | tf_op jit(solution)/shard_map/dot_general | solution.py:89
  443.6 0.6 copy-done.7
  444.2 4.5 multiply_reduce_fusion
  448.7 11.7 %all-reduce.1 = bf16[128,4,64]{0,2,1:T(8,128)(2,1)S(1)} all-reduce(f32[128,4,64]{0,2,1:T(8,128)S(1)} %multiply_reduce_fusion), channel_id=1, replica_groups=mesh['dp'=8,'mp'=4] {'mp'}, use_global_device_ids=true, to_apply=%region_9.11 | all-reduce | flops 32768 | bytes 196608 | tf_op jit(solution)/shard_map/psum | solution.py:103
  460.5 107.8 %reduce-scatter.2.cloned.1.call-done = f32[128,4,2048]{2,0,1:T(8,128)} async-done(((f32[128,4,8192]{2,0,1:T(8,128)}), f32[128,4,2048]{2,0,1:T(8,128)}) %reduce-scatter.2.cloned.1.call-update) | async-done | bytes 4194320 | tf_op jit(solution)/shard_map/reduce_scatter | solution.py:112
  568.3 5.9 %add_convert_fusion = bf16[128,4,2048]{2,0,1:T(8,128)(2,1)S(1)} fusion(f32[128,4,2048]{2,0,1:T(8,128)} %reduce-scatter.2.cloned.1.call-done, bf16[16,64,2048]{2,1,0:T(8,128)(2,1)} %all-gather.5.cloned.1.call-done, bf16[128,16]{0,1:T(8,128)(2,1)S(1)} %get-tuple-element.15, bf16[128,4,64]{0,2,1:T(8,128)(2,1)S(1)} %all-reduce.1), kind=kOutput, calls=%fused_computation.19 | convolution fusion | flops 2153250816 | bytes 10555392 | tf_op jit(solution)/shard_map/utja,jam->utm/dot_general | solution.py:108
  574.2 2.9 copy.104
  (54 shorter events, 4.0 us)
Async XLA Ops:
  7.4 1.0 copy-start
  57.7 254.4 %all-to-all-start.1 = ((bf16[8,64,2,2,16,128]{5,4,3,2,1,0:T(8,128)(2,1)}), bf16[8,64,2,2,16,128]{5,4,3,2,1,0:T(8,128)(2,1)}, u32[]{:S(2)}, u32[]{:S(2)}) async-start(bf16[8,64,2,2,16,128]{5,4,3,2,1,0:T(8,128)(2,1)} %bitcast.87), calls=%async_computation.1 | async-start | bytes 16777216 | tf_op jit(solution)/shard_map/all_to_all | solution.py:52
  62.7 381.5 %all-gather.3.cloned.1.call-start = ((), (), s32[]{:S(2)}) async-start(), calls=%async_computation.4 | async-start | bytes 4718592 | tf_op jit(solution)/shard_map/all_gather | solution.py:96
  63.4 397.0 %all-gather.5.cloned.1.call-start = ((), (), s32[]{:S(2)}) async-start(), calls=%async_computation.5 | async-start | bytes 4718592 | tf_op jit(solution)/shard_map/all_gather | solution.py:104
  64.2 3.4 copy-start.5
  64.2 504.1 %reduce-scatter.2.cloned.1.call-start = ((), (), s32[]{:S(2)}) async-start(), calls=%async_computation.3 | async-start | bytes 20971520 | tf_op jit(solution)/shard_map/reduce_scatter | solution.py:112
  68.0 11.5 %copy-start.8 = (s32[128]{0:T(128)S(1)}, s32[128]{0:T(128)}, u32[]{:S(2)}) copy-start(s32[128]{0:T(128)} %param.17) | copy-start | bytes 1540
  374.5 4.4 copy-start.3
  403.4 7.0 %copy-start.2 = (f32[128,4,2,8,4]{3,4,1,2,0:T(4,128)S(1)}, f32[128,4,2,8,4]{3,4,1,2,0:T(4,128)}, u32[]{:S(2)}) copy-start(f32[128,4,2,8,4]{3,4,1,2,0:T(4,128)} %get-tuple-element.17) | copy-start | bytes 393220
  403.4 7.0 %copy-start.4 = (f32[128,4,2,8]{3,1,2,0:T(4,128)S(1)}, f32[128,4,2,8]{3,1,2,0:T(4,128)}, u32[]{:S(2)}) copy-start(f32[128,4,2,8]{3,1,2,0:T(4,128)} %copy-done.3) | copy-start | bytes 98308
  403.5 7.0 %copy-start.6 = (f32[128,4,2,8]{3,1,2,0:T(4,128)S(1)}, f32[128,4,2,8]{3,1,2,0:T(4,128)}, u32[]{:S(2)}) copy-start(f32[128,4,2,8]{3,1,2,0:T(4,128)} %copy.99) | copy-start | bytes 98308
  443.5 0.7 copy-start.7
  568.3 8.8 %copy-start.1 = (s32[4096]{0:T(1024)S(1)}, s32[4096]{0:T(1024)}, u32[]{:S(2)}) copy-start(s32[4096]{0:T(1024)} %param.15) | copy-start | bytes 49156
Sparse Core Ops, SparseCore 0:
  65.9 202.7 all-gather.2
  271.0 83.5 all-gather.4
Sparse Core Ops, SparseCore 1:
  443.7 124.6 reduce-scatter.1
where the time goes:
time: 592 us; the launch traced here: 585 us
  waiting for transfers between devices  342 us (58%)
  local copies, waits for them, and re-layouts  102 us (17%)
  matrix products  75.1 us (13%)
  blocking collectives  25.2 us (4%)
  other arithmetic  19.7 us (3%)
  between operations  15.4 us (3%)
    all_to_all x1, waiting for transfers between devices, shards(): lax.all_to_all(served, 'dp', split_axis=0, concat_axis=0, tiled=True)  233 us
    reduce_scatter x1, waiting for transfers between devices, shards(): lax.psum_scatter(base_product, 'mp', scatter_dimension=2, tiled=True)  108 us
    dot_general x1, matrix products, shards(): jnp.dot(attended.reshape(req_dev * step_count, query_width), output_weigh...  27 us
    gather x1, local copies, waits for them, and re-layouts, shards(): own_blocks = jnp.take(flat_rows, target * capacity + slot_index, axis=0)  23.6 us
    gather x1, local copies, waits for them, and re-layouts, shards(): jnp.take(key_value_pool, wanted.reshape(-1), axis=0)  22.9 us
    convert_element_type x1, local copies, waits for them, and re-layouts, shards(): prefix_p = (prefix_w / row_total[..., None, None]).astype(jnp.bfloat16)  22.9 us
    dot_general x1, matrix products, shards(): jnp.einsum('qsghd,qbgtd->qsghbt', query, own_blocks[:, :, 0], preferred_e...  17.3 us
    all_to_all x1, blocking collectives, shards(): lax.all_to_all(wish_table, 'dp', split_axis=0, concat_axis=0, tiled=True)  13.5 us
  transfers between devices with their start and end apart: 4, of which 2 were waited for; matrix products, arithmetic and copies ran while one was open for 26% of the time, Pallas kernels for 0%

commit v1 on v0

--- a/solution.py
+++ b/solution.py
@@ -45,7 +45,19 @@
     wish_table = jnp.sum(
         jnp.where(key[:, None] == table_ids[None, :], local_slot[:, None], 0), axis=0
     ).reshape(owners, capacity)
-    wanted = lax.all_to_all(wish_table, "dp", split_axis=0, concat_axis=0, tiled=True)
+    ways, here = (lax.axis_size("dp"), lax.axis_index("dp"))
+    width = wish_table.shape[0] // ways
+    shape = list(wish_table.shape)
+    shape[0] = width
+    height = shape[0]
+    shape[0] = height * ways
+    full = jnp.zeros(shape, wish_table.dtype)
+    for mask in range(ways):
+        part = lax.dynamic_slice_in_dim(wish_table, (here ^ mask) * width, width, axis=0)
+        if mask:
+            part = lax.ppermute(part, "dp", [(d, d ^ mask) for d in range(ways)])
+        full = lax.dynamic_update_slice_in_dim(full, part, (here ^ mask) * height, axis=0)
+    wanted = full
     served = jnp.take(key_value_pool, wanted.reshape(-1), axis=0).reshape(
         (owners, capacity) + key_value_pool.shape[1:]
     )

time: 592 us -> 595 us (level)
  blocking collectives: 25.2 us -> 11.7 us
  starting transfers between devices: 5.26 us -> 17.8 us
    all_to_all x1 -> x0, blocking collectives: 13.5 us -> none  [shards(): lax.all_to_all(wish_table, 'dp', split_axis=0, concat_axis=0, tiled=True)]
    ppermute x0 -> x7, starting transfers between devices: none -> 12.6 us  [shards(): part = lax.ppermute(part, 'dp', [(d, d ^ mask) for d in range(ways)])]
    ppermute x0 -> x7, waiting for transfers between devices: none -> 6.05 us  [shards(): part = lax.ppermute(part, 'dp', [(d, d ^ mask) for d in range(ways)])]
  transfers between devices with their start and end apart: 4 -> 11, of which waited for: 2 -> 5; matrix products, arithmetic and copies ran while one was open for 26% -> 26% of each run, Pallas kernels for 0% -> 0%
where the time goes in v1:
time: 595 us; the launch traced here: 588 us
  waiting for transfers between devices  346 us (58%)
  local copies, waits for them, and re-layouts  102 us (17%)
  matrix products  75.3 us (13%)
  other arithmetic  19.1 us (3%)
  starting transfers between devices  17.8 us (3%)
  between operations  15.4 us (3%)
  blocking collectives  11.7 us (2%)
    all_to_all x1, waiting for transfers between devices, shards(): lax.all_to_all(served, 'dp', split_axis=0, concat_axis=0, tiled=True)  231 us
    reduce_scatter x1, waiting for transfers between devices, shards(): lax.psum_scatter(base_product, 'mp', scatter_dimension=2, tiled=True)  108 us
    dot_general x1, matrix products, shards(): jnp.dot(attended.reshape(req_dev * step_count, query_width), output_weigh...  27 us
    gather x1, local copies, waits for them, and re-layouts, shards(): own_blocks = jnp.take(flat_rows, target * capacity + slot_index, axis=0)  23.6 us
    gather x1, local copies, waits for them, and re-layouts, shards(): jnp.take(key_value_pool, wanted.reshape(-1), axis=0)  22.9 us
    convert_element_type x1, local copies, waits for them, and re-layouts, shards(): prefix_p = (prefix_w / row_total[..., None, None]).astype(jnp.bfloat16)  22.9 us
    dot_general x1, matrix products, shards(): jnp.einsum('qsghd,qbgtd->qsghbt', query, own_blocks[:, :, 0], preferred_e...  17.3 us
    ppermute x7, starting transfers between devices, shards(): part = lax.ppermute(part, 'dp', [(d, d ^ mask) for d in range(ways)])  12.6 us
  transfers between devices with their start and end apart: 11, of which 5 were waited for; matrix products, arithmetic and copies ran while one was open for 26% of the time, Pallas kernels for 0%

profile of v1, /device:TPU:0, one launch (start us, length us, event | category | flops | bytes accessed | tf_op | source)
XLA Modules:
  0.0 587.7 jit_solution(1663309792171998617)
XLA Ops:
  7.4 0.8 copy.87
  8.5 3.1 gather_fusion
  12.5 3.0 collective-permute-start
  15.5 1.6 collective-permute-start.1
  17.1 3.0 collective-permute-start.3
  20.1 1.3 collective-permute-start.4
  21.4 3.7 collective-permute-start.5
  25.4 1.3 collective-permute-done.5
  26.8 4.6 collective-permute-done.6
  31.5 22.9 %gather_fusion.1 = bf16[512,2,2,16,128]{4,3,2,1,0:T(8,128)(2,1)} fusion(bf16[512,2,2,16,128]{4,3,2,1,0:T(8,128)(2,1)} %param.14, s32[1024]{0:T(1024)S(1)} %pad_clamp_fusion.1), kind=kCustom, calls=%fused_computation.clone | custom fusion | bytes 16779264 | tf_op jit(solution)/shard_map/jit(_take)/gather | solution.py:61
  54.4 7.6 %broadcast_select_fusion.1 = bf16[512,2,2,16,128]{4,3,2,1,0:T(8,128)(2,1)} fusion(bf16[512,2,2,16,128]{4,3,2,1,0:T(8,128)(2,1)} %gather_fusion.1, pred[512]{0:T(512)(128)(4,1)S(1)} %compare_and_fusion.3), kind=kLoop, calls=%fused_computation.6 | loop fusion | flops 4194304 | bytes 16777728 | tf_op jit(solution)/shard_map/jit(_take)/select_n | solution.py:61
  62.0 4.9 all-to-all-start
  68.7 3.2 reshape.274
  72.2 10.8 %fusion.37 = (f32[128,4,2,8]{3,1,2,0:T(4,128)S(1)}, f32[128,4,2,8,4]{3,4,1,2,0:T(4,128)}) fusion(bf16[128,4,2,8,128]{4,3,2,1,0:T(8,128)(2,1)S(1)} %reshape.274, bf16[128,4,1,2,128]{4,3,2,1,0:T(2,128)(2,1)S(1)} %get-tuple-element.13, pred[4,4]{1,0:T(4,128)(4,1)S(1)} %iota_compare_fusion.3), kind=kOutput, calls=%fused_computation.87 | convolution fusion | flops 8478720 | bytes 2523152 | tf_op jit(solution)/shard_map/qsghd,qjgd->qsghj/dot_general | solution.py:81
  83.8 231.2 %all-to-all-done = bf16[8,64,2,2,16,128]{5,4,3,2,1,0:T(8,128)(2,1)} async-done(((bf16[8,64,2,2,16,128]{5,4,3,2,1,0:T(8,128)(2,1)}), bf16[8,64,2,2,16,128]{5,4,3,2,1,0:T(8,128)(2,1)}, u32[]{:S(2)}, u32[]{:S(2)}) %all-to-all-start) | async-done | bytes 8388640 | tf_op jit(solution)/shard_map/all_to_all | solution.py:64
  314.9 23.6 %gather_fusion.2 = bf16[512,2,2,16,128]{4,3,2,1,0:T(8,128)(2,1)} fusion(bf16[512,2,2,16,128]{4,3,2,1,0:T(8,128)(2,1)} %bitcast.3, s32[1024]{0:T(1024)S(1)} %pad_clamp_fusion), kind=kCustom, calls=%fused_computation.1.clone | custom fusion | bytes 16779264 | tf_op jit(solution)/shard_map/jit(_take)/gather | solution.py:66
  338.6 4.9 broadcast_select_fusion
  343.5 3.7 fusion.35
  347.2 17.3 %fusion.2 = f32[128,2,4,16,4,8]{3,5,4,2,1,0:T(8,128)} fusion(bf16[128,4,1,2,16,128]{5,4,3,2,1,0:T(8,128)(2,1)S(1)} %get-tuple-element.11, bf16[128,4,2,8,128]{4,3,2,1,0:T(8,128)(2,1)S(1)} %reshape.274), kind=kOutput, calls=%fused_computation.8 | convolution fusion | flops 134217728 | bytes 8388608 | tf_op jit(solution)/shard_map/qsghd,qbgtd->qsghbt/dot_general | solution.py:72
  364.5 12.2 %copy.92 = f32[128,2,4,16,4,8]{0,3,2,5,1,4:T(8,128)S(1)} copy(f32[128,2,4,16,4,8]{3,5,4,2,1,0:T(8,128)} %fusion.2) | data formatting | bytes 4194304 | tf_op jit(solution)/shard_map/qsghd,qbgtd->qsghbt/dot_general | solution.py:72
  377.3 3.6 fusion.22
  381.8 1.1 copy.99
  383.4 22.9 %copy.98 = bf16[128,4,2,8,4,16]{5,3,4,1,2,0:T(8,128)(2,1)} copy(bf16[128,4,2,8,4,16]{0,5,4,3,2,1:T(8,128)(2,1)S(1)} %divide_convert_fusion) | data formatting | bytes 2097152 | tf_op jit(solution)/shard_map/convert_element_type | solution.py:92
  406.3 7.0 %fusion.3 = f32[128,2,128,4,8,1]{2,4,5,3,1,0:T(8,128)S(1)} fusion(bf16[128,4,2,8,4,16]{5,3,4,1,2,0:T(8,128)(2,1)} %copy.98, bf16[128,4,1,2,16,128]{5,4,3,2,1,0:T(8,128)(2,1)} %get-tuple-element.10), kind=kOutput, calls=%fused_computation.10 | convolution fusion | flops 134217728 | bytes 9437184 | tf_op jit(solution)/shard_map/qsghbt,qbgtd->qsghd/dot_general | solution.py:94
  413.4 2.6 fusion.4
  416.0 3.4 copy.101
  419.4 27.0 %fusion = f32[128,4,8192]{2,0,1:T(8,128)} fusion(bf16[128,4,2048]{0,2,1:T(8,128)(2,1)S(1)} %bitcast.89, bf16[2048,8192]{1,0:T(8,128)(2,1)} %param.19), kind=kOutput, calls=%fused_computation.3 | convolution fusion | flops 17179869184 | bytes 52428800 | tf_op jit(solution)/shard_map/dot_general | solution.py:101
  447.2 4.5 multiply_reduce_fusion
  451.7 11.7 %all-reduce.1 = bf16[128,4,64]{0,2,1:T(8,128)(2,1)S(1)} all-reduce(f32[128,4,64]{0,2,1:T(8,128)S(1)} %multiply_reduce_fusion), channel_id=1, replica_groups=mesh['dp'=8,'mp'=4] {'mp'}, use_global_device_ids=true, to_apply=%region_9.11 | all-reduce | flops 32768 | bytes 196608 | tf_op jit(solution)/shard_map/psum | solution.py:115
  463.4 107.8 %reduce-scatter.2.cloned.1.call-done = f32[128,4,2048]{2,0,1:T(8,128)} async-done(((f32[128,4,8192]{2,0,1:T(8,128)}), f32[128,4,2048]{2,0,1:T(8,128)}) %reduce-scatter.2.cloned.1.call-update) | async-done | bytes 4194320 | tf_op jit(solution)/shard_map/reduce_scatter | solution.py:124
  571.2 5.9 add_convert_fusion
  577.1 2.9 copy.104
  (75 shorter events, 7.1 us)
Async XLA Ops:
  7.4 1.1 copy-start
  12.5 8.9 %collective-permute-start = (s32[1,64]{1,0:T(1,128)S(1)}, s32[1,64]{1,0:T(1,128)S(1)}, u32[]{:S(2)}, u32[]{:S(2)}) collective-permute-start(s32[1,64]{1,0:T(1,128)S(1)} %get-tuple-element.20), channel_id=1, source_target_pairs={{0,4},{4,0},{8,12},{12,8},{16,20},{20,16},{24,28},{28,24},{1,5},{5... | collective-permute-start | bytes 776 | tf_op jit(solution)/shard_map/ppermute | solution.py:58
  15.5 9.6 %collective-permute-start.1 = (s32[1,64]{1,0:T(1,128)S(1)}, s32[1,64]{1,0:T(1,128)S(1)}, u32[]{:S(2)}, u32[]{:S(2)}) collective-permute-start(s32[1,64]{1,0:T(1,128)S(1)} %get-tuple-element.19), channel_id=1, source_target_pairs={{0,8},{4,12},{8,0},{12,4},{16,24},{20,28},{24,16},{28,20},{1,9},{5... | collective-permute-start | bytes 776 | tf_op jit(solution)/shard_map/ppermute | solution.py:58
  17.1 8.1 %collective-permute-start.2 = (s32[1,64]{1,0:T(1,128)S(1)}, s32[1,64]{1,0:T(1,128)S(1)}, u32[]{:S(2)}, u32[]{:S(2)}) collective-permute-start(s32[1,64]{1,0:T(1,128)S(1)} %get-tuple-element.18), channel_id=1, source_target_pairs={{0,12},{4,8},{8,4},{12,0},{16,28},{20,24},{24,20},{28,16},{1,13},{... | collective-permute-start | bytes 776 | tf_op jit(solution)/shard_map/ppermute | solution.py:58
  17.1 8.2 %collective-permute-start.3 = (s32[1,64]{1,0:T(1,128)S(1)}, s32[1,64]{1,0:T(1,128)S(1)}, u32[]{:S(2)}, u32[]{:S(2)}) collective-permute-start(s32[1,64]{1,0:T(1,128)S(1)} %get-tuple-element.17), channel_id=1, source_target_pairs={{0,16},{4,20},{8,24},{12,28},{16,0},{20,4},{24,8},{28,12},{1,17},{... | collective-permute-start | bytes 776 | tf_op jit(solution)/shard_map/ppermute | solution.py:58
  20.1 5.3 collective-permute-start.4
  21.4 5.4 collective-permute-start.5
  25.1 6.3 %collective-permute-start.6 = (s32[1,64]{1,0:T(1,128)S(1)}, s32[1,64]{1,0:T(1,128)S(1)}, u32[]{:S(2)}, u32[]{:S(2)}) collective-permute-start(s32[1,64]{1,0:T(1,128)S(1)} %get-tuple-element.14), channel_id=1, source_target_pairs={{0,28},{4,24},{8,20},{12,16},{16,12},{20,8},{24,4},{28,0},{1,29},{... | collective-permute-start | bytes 776 | tf_op jit(solution)/shard_map/ppermute | solution.py:58
  62.0 253.0 %all-to-all-start = ((bf16[8,64,2,2,16,128]{5,4,3,2,1,0:T(8,128)(2,1)}), bf16[8,64,2,2,16,128]{5,4,3,2,1,0:T(8,128)(2,1)}, u32[]{:S(2)}, u32[]{:S(2)}) async-start(bf16[8,64,2,2,16,128]{5,4,3,2,1,0:T(8,128)(2,1)} %bitcast.87), calls=%async_computation | async-start | bytes 16777216 | tf_op jit(solution)/shard_map/all_to_all | solution.py:64
  66.9 380.2 %all-gather.3.cloned.1.call-start = ((), (), s32[]{:S(2)}) async-start(), calls=%async_computation.3 | async-start | bytes 4718592 | tf_op jit(solution)/shard_map/all_gather | solution.py:108
  67.7 395.7 %all-gather.5.cloned.1.call-start = ((), (), s32[]{:S(2)}) async-start(), calls=%async_computation.4 | async-start | bytes 4718592 | tf_op jit(solution)/shard_map/all_gather | solution.py:116
  68.4 3.4 copy-start.5
  68.4 502.8 %reduce-scatter.2.cloned.1.call-start = ((), (), s32[]{:S(2)}) async-start(), calls=%async_computation.2 | async-start | bytes 20971520 | tf_op jit(solution)/shard_map/reduce_scatter | solution.py:124
  72.2 11.5 %copy-start.8 = (s32[128]{0:T(128)S(1)}, s32[128]{0:T(128)}, u32[]{:S(2)}) copy-start(s32[128]{0:T(128)} %param.17) | copy-start | bytes 1540
  377.3 4.4 copy-start.3
  406.3 7.0 %copy-start.2 = (f32[128,4,2,8,4]{3,4,1,2,0:T(4,128)S(1)}, f32[128,4,2,8,4]{3,4,1,2,0:T(4,128)}, u32[]{:S(2)}) copy-start(f32[128,4,2,8,4]{3,4,1,2,0:T(4,128)} %get-tuple-element.25) | copy-start | bytes 393220
  406.3 7.0 %copy-start.4 = (f32[128,4,2,8]{3,1,2,0:T(4,128)S(1)}, f32[128,4,2,8]{3,1,2,0:T(4,128)}, u32[]{:S(2)}) copy-start(f32[128,4,2,8]{3,1,2,0:T(4,128)} %copy-done.3) | copy-start | bytes 98308
  406.3 7.0 %copy-start.6 = (f32[128,4,2,8]{3,1,2,0:T(4,128)S(1)}, f32[128,4,2,8]{3,1,2,0:T(4,128)}, u32[]{:S(2)}) copy-start(f32[128,4,2,8]{3,1,2,0:T(4,128)} %copy.99) | copy-start | bytes 98308
  446.5 0.7 copy-start.7
  571.2 8.8 %copy-start.1 = (s32[4096]{0:T(1024)S(1)}, s32[4096]{0:T(1024)}, u32[]{:S(2)}) copy-start(s32[4096]{0:T(1024)} %param.15) | copy-start | bytes 49156
Sparse Core Ops, SparseCore 0:
  70.1 201.3 all-gather.2
  273.9 83.5 all-gather.4
Sparse Core Ops, SparseCore 1:
  446.6 124.6 reduce-scatter.1
